TPU v7x, 32 devices: a whole 2x2x4 slice. The times are simulated.
32 devices in a mesh: row: 8 (over z, y), rep: 4 (over x, core).
Axes of the slice: x: 2, y: 2, z: 4, core: 2. Of those that a mesh axis runs over, the one named last changes fastest.
Arguments:
- features: bfloat16 [2048, 256], P('row'), may hold values from -6 to 6
- cotangent: bfloat16 [2048, 256], P('row'), may hold values from -0.3125 to 0.3125
- weight_one: bfloat16 [256, 256], replicated, may hold values from -0.375 to 0.375
- weight_two: bfloat16 [256, 256], replicated, may hold values from -0.375 to 0.375
- block_index: int32 [8, 4, 2, 4], P('row', 'rep'), may hold values from 0 to 15, as said below
- block_count: int32 [8, 4, 2], P('row', 'rep'), may hold values from 0 to 4
- block_values: bfloat16 [8, 4, 2, 4, 128, 128], P('row', 'rep'), as said below
Outputs:
- logits: bfloat16 [2048, 256], P(('row', 'rep'))
- grad_one: float32 [256, 256], replicated
- grad_two: float32 [256, 256], replicated
Inputs may be any that keep to these rules, and one draw needn't show every extreme that they name: block_index[i, j, a, s] lies in [j * 4, (j + 1) * 4); for s < block_count[i, j, a] the entries rise strictly; later entries equal j * 4 and are not part of A. `block_values`: A is symmetric: block (r, c) is listed exactly when block (c, r) is, and its entries are the transpose of those of block (c, r). Entries are normal with standard deviation (0.5 * 128 * 16) ** -0.5, cut at five such deviations; blocks on the diagonal are symmetric.
All inputs are finite; a program needn't handle non-finite values.
Results may differ from a plain program's by a relative error of at most 0.0059.
Values may be sent and summed in bfloat16 or wider, within the bound.
No kernel may reach another device: no remote copies, remote signals or barrier semaphores. Data moves between devices by JAX's collectives and lax.ppermute only.
A program may use at most 64 MiB of HBM per device.

v0:
```python
import jax
import jax.numpy as jnp
from jax import lax
from jax.sharding import PartitionSpec as P


def broadcast(array, axis, root):
    mine = lax.axis_index(axis) == root
    return lax.psum(jnp.where(mine, array, jnp.zeros_like(array)), axis)


def aggregate(source, block_index, block_count, block_values):
    copies = lax.axis_size("rep")
    sections = lax.axis_size("row") // copies
    copy_index = lax.axis_index("rep")
    node_rows, feature_width = source.shape
    block_rows = block_values.shape[2]
    slot_count = block_values.shape[3]
    block_side = block_values.shape[-1]

    def fetch(state_unused, section_index):
        panel = broadcast(source, "row", copy_index * sections + section_index)
        return (state_unused, panel)

    state_unused, panels = lax.scan(fetch, jnp.int32(0), jnp.arange(sections, dtype=jnp.int32))
    panels = panels.reshape(sections * block_rows, block_side, feature_width)
    columns = block_index[0, 0] - copy_index * slot_count
    live_slots = jnp.arange(slot_count, dtype=jnp.int32)[None, :] < block_count[0, 0][:, None]
    picked = jnp.take(panels, columns.reshape(-1), axis=0).reshape(
        block_rows, slot_count, block_side, feature_width
    )
    picked = jnp.where(live_slots[:, :, None, None], picked, jnp.zeros((), picked.dtype))
    partial_value = lax.dot_general(
        block_values[0, 0],
        picked,
        (((1, 3), (1, 2)), ((0,), (0,))),
        preferred_element_type=jnp.float32,
    )
    partial_value = partial_value.reshape(node_rows, feature_width)
    result = lax.psum(partial_value, "rep")
    return result


def shards(features, cotangent, weight_one, weight_two, block_index, block_count, block_values):
    copies = lax.axis_size("rep")
    copy_index = lax.axis_index("rep")
    node_rows = features.shape[0]
    share_rows = node_rows // copies
    first_row = copy_index * share_rows

    def own_rows(array):
        return lax.dynamic_slice_in_dim(array, first_row, share_rows, 0)

    agg_one = aggregate(features, block_index, block_count, block_values).astype(jnp.bfloat16)
    pre_one = jnp.dot(agg_one, weight_one, preferred_element_type=jnp.float32)
    hidden = jax.nn.silu(pre_one).astype(jnp.bfloat16)
    agg_two = aggregate(hidden, block_index, block_count, block_values).astype(jnp.bfloat16)
    agg_two_own = own_rows(agg_two)
    logits = jnp.dot(agg_two_own, weight_two, preferred_element_type=jnp.float32).astype(
        jnp.bfloat16
    )
    cotangent_own = own_rows(cotangent)
    grad_two = lax.dot_general(
        agg_two_own, cotangent_own, (((0,), (0,)), ((), ())), preferred_element_type=jnp.float32
    )
    grad_two = lax.psum(grad_two, ("row", "rep"))
    back_signal = lax.dot_general(
        cotangent, weight_two, (((1,), (1,)), ((), ())), preferred_element_type=jnp.float32
    ).astype(jnp.bfloat16)
    carried = aggregate(back_signal, block_index, block_count, block_values)
    carried = own_rows(carried)
    pre_own = own_rows(pre_one)
    agg_one_own = own_rows(agg_one)
    gate_value = jax.nn.sigmoid(pre_own)
    pre_grad = (carried * (gate_value + pre_own * gate_value * (1.0 - gate_value))).astype(
        jnp.bfloat16
    )
    grad_one = lax.dot_general(
        agg_one_own, pre_grad, (((0,), (0,)), ((), ())), preferred_element_type=jnp.float32
    )
    grad_one = lax.psum(grad_one, ("row", "rep"))
    return (logits, grad_one, grad_two)


def solution(mesh):
    in_specs = (
        P("row", None),
        P("row", None),
        P(),
        P(),
        P("row", "rep", None, None),
        P("row", "rep", None),
        P("row", "rep", None, None, None, None),
    )
    out_specs = (P(("row", "rep"), None), P(), P())
    return jax.shard_map(shards, mesh=mesh, in_specs=in_specs, out_specs=out_specs, check_vma=False)
```

profile of v0, /device:TPU:0, one launch (start us, length us, event | category | flops | bytes accessed | tf_op | source)
XLA Modules:
  0.0 661.8 jit_solution(11847135036822304722)
XLA Ops:
  8.9 1.2 convolution_convert_fusion
  10.1 154.0 %while.38 = (s32[]{:T(128)}, bf16[2,256,256]{2,1,0:T(8,128)(2,1)S(1)}, s32[2]{0:T(128)S(1)}, s32[]{:T(128)}, bf16[256,256]{1,0:T(8,128)(2,1)S(1)}, /*index=5*/s32[]{:T(128)}, u32[]{:T(128)}, u32[]{:T(128)}) while((s32[]{:T(128)}, bf16[2,256,256]{2,1,0:T(8,128)(2,1)S(1)}, s32[2]{0:T(128)S(1)}, s32[]{:T(128)}, ...), condition=%wide.region_10.12_spmd, body=%wide.region_8.11_spmd.sunk | while | flops 131079 | bytes 1310923 | solution.py:25
  12.1 75.9 %all-reduce.17.cloned.1.call-done = bf16[1,256,256]{2,1,0:T(8,128)(2,1)} async-done(((bf16[1,256,256]{2,1,0:T(8,128)(2,1)}), bf16[1,256,256]{2,1,0:T(8,128)(2,1)}) %all-reduce.17.cloned.1.call-update) | async-done | bytes 131088 | tf_op jit(solution)/shard_map/while/body/eval_jaxpr/psum | solution.py:9
  88.0 0.9 constant_dynamic-update-slice_fusion.8
  90.9 72.3 %all-reduce.17.cloned.1.call-done = bf16[1,256,256]{2,1,0:T(8,128)(2,1)} async-done(((bf16[1,256,256]{2,1,0:T(8,128)(2,1)}), bf16[1,256,256]{2,1,0:T(8,128)(2,1)}) %all-reduce.17.cloned.1.call-update) | async-done | bytes 131088 | tf_op jit(solution)/shard_map/while/body/eval_jaxpr/psum | solution.py:9
  163.2 0.9 constant_dynamic-update-slice_fusion.8
  165.6 150.0 %while.36 = (s32[]{:T(128)}, bf16[2,256,256]{2,1,0:T(8,128)(2,1)S(1)}, s32[2]{0:T(128)S(1)}, s32[]{:T(128)}, bf16[256,256]{1,0:T(8,128)(2,1)S(1)}, /*index=5*/s32[]{:T(128)}, u32[]{:T(128)}, u32[]{:T(128)}) while((s32[]{:T(128)}, bf16[2,256,256]{2,1,0:T(8,128)(2,1)S(1)}, s32[2]{0:T(128)S(1)}, s32[]{:T(128)}, bf16[256,256]{1,0:T(8,128)(2,1)S(1)}, ...), condition=%wide.region_2.3_spmd, body=%wide.region_0.2_spmd.sunk | while | flops 131079 | bytes 1310923 | solution.py:25
  167.5 72.3 %all-reduce.13.cloned.1.call-done = bf16[1,256,256]{2,1,0:T(8,128)(2,1)} async-done(((bf16[1,256,256]{2,1,0:T(8,128)(2,1)}), bf16[1,256,256]{2,1,0:T(8,128)(2,1)}) %all-reduce.13.cloned.1.call-update) | async-done | bytes 131088 | tf_op jit(solution)/shard_map/while/body/eval_jaxpr/psum | solution.py:9
  239.8 0.9 constant_dynamic-update-slice_fusion.6
  242.8 71.9 %all-reduce.13.cloned.1.call-done = bf16[1,256,256]{2,1,0:T(8,128)(2,1)} async-done(((bf16[1,256,256]{2,1,0:T(8,128)(2,1)}), bf16[1,256,256]{2,1,0:T(8,128)(2,1)}) %all-reduce.13.cloned.1.call-update) | async-done | bytes 131088 | tf_op jit(solution)/shard_map/while/body/eval_jaxpr/psum | solution.py:9
  314.7 0.9 constant_dynamic-update-slice_fusion.6
  317.4 13.1 %all-reduce.18 = bf16[256,256]{1,0:T(8,128)(2,1)S(1)} all-reduce(f32[256,256]{1,0:T(8,128)S(1)} %bitcast.65), channel_id=1, replica_groups=mesh['row'=8,'rep'=4] {'rep'}, use_global_device_ids=true, to_apply=%region_3.5 | all-reduce | flops 65536 | bytes 393216 | tf_op jit(solution)/shard_map/psum | solution.py:40
  330.5 1.0 fusion
  331.8 150.5 %while.37 = (s32[]{:T(128)}, bf16[2,256,256]{2,1,0:T(8,128)(2,1)S(1)}, s32[2]{0:T(128)S(1)}, s32[]{:T(128)}, bf16[256,256]{1,0:T(8,128)(2,1)S(1)}, /*index=5*/s32[]{:T(128)}, u32[]{:T(128)}, u32[]{:T(128)}) while((s32[]{:T(128)}, bf16[2,256,256]{2,1,0:T(8,128)(2,1)S(1)}, s32[2]{0:T(128)S(1)}, s32[]{:T(128)}, bf16[256,256]{1,0:T(8,128)(2,1)S(1)}, ...), condition=%wide.region_6.8_spmd, body=%wide.region_4.7_spmd.sunk | while | flops 131079 | bytes 1310923 | solution.py:25
  333.8 72.7 %all-reduce.15.cloned.1.call-done = bf16[1,256,256]{2,1,0:T(8,128)(2,1)} async-done(((bf16[1,256,256]{2,1,0:T(8,128)(2,1)}), bf16[1,256,256]{2,1,0:T(8,128)(2,1)}) %all-reduce.15.cloned.1.call-update) | async-done | bytes 131088 | tf_op jit(solution)/shard_map/while/body/eval_jaxpr/psum | solution.py:9
  406.5 0.9 constant_dynamic-update-slice_fusion.7
  409.5 71.9 %all-reduce.15.cloned.1.call-done = bf16[1,256,256]{2,1,0:T(8,128)(2,1)} async-done(((bf16[1,256,256]{2,1,0:T(8,128)(2,1)}), bf16[1,256,256]{2,1,0:T(8,128)(2,1)}) %all-reduce.15.cloned.1.call-update) | async-done | bytes 131088 | tf_op jit(solution)/shard_map/while/body/eval_jaxpr/psum | solution.py:9
  481.4 0.9 constant_dynamic-update-slice_fusion.7
  484.0 13.8 %all-reduce.19 = bf16[256,256]{1,0:T(8,128)(2,1)S(1)} all-reduce(f32[256,256]{1,0:T(8,128)S(1)} %bitcast.64), channel_id=1, replica_groups=mesh['row'=8,'rep'=4] {'rep'}, use_global_device_ids=true, to_apply=%region_7.9 | all-reduce | flops 65536 | bytes 393216 | tf_op jit(solution)/shard_map/psum | solution.py:40
  497.7 1.7 fusion.16
  499.4 17.9 %all-reduce.9.cloned.1.call-done = f32[256,256]{1,0:T(8,128)} async-done(((f32[256,256]{1,0:T(8,128)}), f32[256,256]{1,0:T(8,128)}) %all-reduce.9.cloned.1.call-update) | async-done | bytes 262160 | tf_op jit(solution)/shard_map/psum | solution.py:40
  517.3 1.8 fusion.15
  520.7 131.2 %all-reduce.11.cloned.1.call-done = (f32[256,256]{1,0:T(8,128)}, f32[256,256]{1,0:T(8,128)}) async-done(((f32[256,256]{1,0:T(8,128)}, f32[256,256]{1,0:T(8,128)}), (f32[256,256]{1,0:T(8,128)}, f32[256,256]{1,0:T(8,128)})) %all-reduce.11.cloned.1.call-update) | async-done | bytes 524304 | tf_op jit(solution)/shard_map/psum | solution.py:81
  651.9 1.7 copy.44
  (64 shorter events, 16.2 us)
Async XLA Ops:
  8.0 309.1 %copy-start = (bf16[1,1,2,4,128,128]{5,4,3,2,1,0:T(8,128)(2,1)S(1)}, bf16[1,1,2,4,128,128]{5,4,3,2,1,0:T(8,128)(2,1)}, u32[]{:S(2)}) copy-start(bf16[1,1,2,4,128,128]{5,4,3,2,1,0:T(8,128)(2,1)} %param.21) | copy-start | bytes 786436
  8.0 0.7 copy-start.4
  10.1 77.9 %all-reduce.17.cloned.1.call-start = ((), (), s32[]{:S(2)}) async-start(), calls=%async_computation.4 | async-start | bytes 262144 | tf_op jit(solution)/shard_map/while/body/eval_jaxpr/psum | solution.py:9
  88.9 74.3 %all-reduce.17.cloned.1.call-start = ((), (), s32[]{:S(2)}) async-start(), calls=%async_computation.4 | async-start | bytes 262144 | tf_op jit(solution)/shard_map/while/body/eval_jaxpr/psum | solution.py:9
  164.7 0.9 copy-start.1
  165.6 74.2 %all-reduce.13.cloned.1.call-start = ((), (), s32[]{:S(2)}) async-start(), calls=%async_computation.2 | async-start | bytes 262144 | tf_op jit(solution)/shard_map/while/body/eval_jaxpr/psum | solution.py:9
  240.8 73.9 %all-reduce.13.cloned.1.call-start = ((), (), s32[]{:S(2)}) async-start(), calls=%async_computation.2 | async-start | bytes 262144 | tf_op jit(solution)/shard_map/while/body/eval_jaxpr/psum | solution.py:9
  316.2 0.7 copy-start.6
  330.5 1.0 copy-start.5
  331.8 74.7 %all-reduce.15.cloned.1.call-start = ((), (), s32[]{:S(2)}) async-start(), calls=%async_computation.3 | async-start | bytes 262144 | tf_op jit(solution)/shard_map/while/body/eval_jaxpr/psum | solution.py:9
  407.5 73.9 %all-reduce.15.cloned.1.call-start = ((), (), s32[]{:S(2)}) async-start(), calls=%async_computation.3 | async-start | bytes 262144 | tf_op jit(solution)/shard_map/while/body/eval_jaxpr/psum | solution.py:9
  482.3 35.0 %all-reduce.9.cloned.1.call-start = ((), (), s32[]{:S(2)}) async-start(), calls=%async_computation | async-start | bytes 524288 | tf_op jit(solution)/shard_map/psum | solution.py:40
  482.9 169.0 %all-reduce.11.cloned.1.call-start = ((), (), s32[]{:S(2)}) async-start(), calls=%async_computation.1 | async-start | bytes 1048576 | tf_op jit(solution)/shard_map/psum | solution.py:81
  519.0 0.9 copy-start.2
  651.9 1.7 copy-start.3
Sparse Core Ops, SparseCore 0:
  14.8 73.1 all-reduce.16
  93.6 69.4 all-reduce.16
  170.3 69.4 all-reduce.12
  245.2 69.4 all-reduce.12
  336.2 70.2 all-reduce.14
  411.9 69.4 all-reduce.14
Sparse Core Ops, SparseCore 1:
  485.7 31.5 all-reduce.8
  523.2 128.7 all-reduce.10
where the time goes:
time: 662 us
  waiting for transfers between devices  587 us (89%)
  blocking collectives  26.8 us (4%)
  local copies, waits for them, and re-layouts  16.4 us (2%)
  between operations  15.7 us (2%)
  matrix products  7.22 us (1%)
    psum x6, waiting for transfers between devices, broadcast(): return lax.psum(jnp.where(mine, array, jnp.zeros_like(array)), axis)  437 us
    psum x1, waiting for transfers between devices, shards(): grad_one = lax.psum(grad_one, ('row', 'rep'))  131 us
    psum x2, blocking collectives, aggregate(): result = lax.psum(partial_value, 'rep')  26.8 us
    psum x1, waiting for transfers between devices, aggregate(): result = lax.psum(partial_value, 'rep')  17.9 us
  transfers between devices with their start and end apart: 8, of which 8 were waited for; matrix products, arithmetic and copies ran while one was open for 1% of the time, Pallas kernels for 0%

commit v1 on v0

--- a/solution.py
+++ b/solution.py
@@ -6,7 +6,7 @@
 
 def broadcast(array, axis, root):
     mine = lax.axis_index(axis) == root
-    return lax.psum(jnp.where(mine, array, jnp.zeros_like(array)), axis)
+    return jnp.sum(lax.all_gather(jnp.where(mine, array, jnp.zeros_like(array)), axis), axis=0)
 
 
 def aggregate(source, block_index, block_count, block_values):

time: 662 us -> 475 us (0.72)
  waiting for transfers between devices: 587 us -> 397 us
  other arithmetic: 4.38 us -> 12.6 us
    psum x6 -> x0, waiting for transfers between devices: 437 us -> none  [broadcast(): return lax.psum(jnp.where(mine, array, jnp.zeros_like(array)), axis)]
    all_gather x0 -> x6, waiting for transfers between devices: none -> 247 us  [broadcast(): lax.all_gather(jnp.where(mine, array, jnp.zeros_like(array)), axis)]
    reduce_sum x0 -> x6, other arithmetic: none -> 8.23 us  [broadcast(): jnp.sum(lax.all_gather(jnp.where(mine, array, jnp.zeros_like(array)), axi...]
where the time goes in v1:
time: 475 us; the launch traced here: 474 us
  waiting for transfers between devices  397 us (84%)
  blocking collectives  26.6 us (6%)
  between operations  15.7 us (3%)
  other arithmetic  12.6 us (3%)
  local copies, waits for them, and re-layouts  11.1 us (2%)
  matrix products  7.22 us (2%)
    all_gather x6, waiting for transfers between devices, broadcast(): lax.all_gather(jnp.where(mine, array, jnp.zeros_like(array)), axis)  247 us
    psum x1, waiting for transfers between devices, shards(): grad_one = lax.psum(grad_one, ('row', 'rep'))  131 us
    psum x2, blocking collectives, aggregate(): result = lax.psum(partial_value, 'rep')  26.6 us
    psum x1, waiting for transfers between devices, aggregate(): result = lax.psum(partial_value, 'rep')  17.7 us
  transfers between devices with their start and end apart: 8, of which 8 were waited for; matrix products, arithmetic and copies ran while one was open for 1% of the time, Pallas kernels for 0%

profile of v1, /device:TPU:0, one launch (start us, length us, event | category | flops | bytes accessed | tf_op | source)
XLA Modules:
  0.0 474.4 jit_solution(16748170341607834419)
XLA Ops:
  8.9 1.2 convolution_convert_fusion
  10.1 91.9 %while.38 = (s32[]{:T(128)}, bf16[2,256,256]{2,1,0:T(8,128)(2,1)S(1)}, s32[2]{0:T(128)S(1)}, s32[]{:T(128)}, bf16[256,256]{1,0:T(8,128)(2,1)S(1)}, /*index=5*/s32[]{:T(128)}, u32[]{:T(128)}, u32[]{:T(128)}, bf16[]{:T(256)}) while((s32[]{:T(128)}, bf16[2,256,256]{2,1,0:T(8,128)(2,1)S(1)}, s32[2]{0:T(128)S(1)}, s32[]{:T(128)}, ...), condition=%wide.region_10.12_spmd, body=%wide.region_8.11_spmd.sunk | while | flops 524295 | bytes 5243093 | solution.py:25
  12.1 44.6 %all-gather.17.cloned.1.call-done = bf16[2048,256]{1,0:T(8,128)(2,1)} async-done(((bf16[256,256]{1,0:T(8,128)(2,1)}), bf16[2048,256]{1,0:T(8,128)(2,1)}) %all-gather.17.cloned.1.call-update) | async-done | bytes 1048592 | tf_op jit(solution)/shard_map/while/body/eval_jaxpr/all_gather | solution.py:9
  56.6 1.4 reduce_sum.41
  60.1 40.5 %all-gather.17.cloned.1.call-done = bf16[2048,256]{1,0:T(8,128)(2,1)} async-done(((bf16[256,256]{1,0:T(8,128)(2,1)}), bf16[2048,256]{1,0:T(8,128)(2,1)}) %all-gather.17.cloned.1.call-update) | async-done | bytes 1048592 | tf_op jit(solution)/shard_map/while/body/eval_jaxpr/all_gather | solution.py:9
  100.6 1.4 reduce_sum.41
  103.5 87.6 %while.36 = (s32[]{:T(128)}, bf16[2,256,256]{2,1,0:T(8,128)(2,1)S(1)}, s32[2]{0:T(128)S(1)}, s32[]{:T(128)}, bf16[256,256]{1,0:T(8,128)(2,1)S(1)}, /*index=5*/s32[]{:T(128)}, u32[]{:T(128)}, u32[]{:T(128)}, bf16[]{:T(256)}) while((s32[]{:T(128)}, bf16[2,256,256]{2,1,0:T(8,128)(2,1)S(1)}, s32[2]{0:T(128)S(1)}, s32[]{:T(128)}, ...), condition=%wide.region_2.3_spmd, body=%wide.region_0.2_spmd.sunk | while | flops 524295 | bytes 5243093 | solution.py:25
  105.5 40.6 %all-gather.13.cloned.1.call-done = bf16[2048,256]{1,0:T(8,128)(2,1)} async-done(((bf16[256,256]{1,0:T(8,128)(2,1)}), bf16[2048,256]{1,0:T(8,128)(2,1)}) %all-gather.13.cloned.1.call-update) | async-done | bytes 1048592 | tf_op jit(solution)/shard_map/while/body/eval_jaxpr/all_gather | solution.py:9
  146.0 1.4 reduce_sum.39
  149.4 40.2 %all-gather.13.cloned.1.call-done = bf16[2048,256]{1,0:T(8,128)(2,1)} async-done(((bf16[256,256]{1,0:T(8,128)(2,1)}), bf16[2048,256]{1,0:T(8,128)(2,1)}) %all-gather.13.cloned.1.call-update) | async-done | bytes 1048592 | tf_op jit(solution)/shard_map/while/body/eval_jaxpr/all_gather | solution.py:9
  189.7 1.4 reduce_sum.39
  192.9 13.1 %all-reduce.9 = bf16[256,256]{1,0:T(8,128)(2,1)S(1)} all-reduce(f32[256,256]{1,0:T(8,128)S(1)} %bitcast.77), channel_id=1, replica_groups=mesh['row'=8,'rep'=4] {'rep'}, use_global_device_ids=true, to_apply=%region_3.5 | all-reduce | flops 65536 | bytes 393216 | tf_op jit(solution)/shard_map/psum | solution.py:40
  206.0 1.0 fusion
  207.2 88.1 %while.37 = (s32[]{:T(128)}, bf16[2,256,256]{2,1,0:T(8,128)(2,1)S(1)}, s32[2]{0:T(128)S(1)}, s32[]{:T(128)}, bf16[256,256]{1,0:T(8,128)(2,1)S(1)}, /*index=5*/s32[]{:T(128)}, u32[]{:T(128)}, u32[]{:T(128)}, bf16[]{:T(256)}) while((s32[]{:T(128)}, bf16[2,256,256]{2,1,0:T(8,128)(2,1)S(1)}, s32[2]{0:T(128)S(1)}, s32[]{:T(128)}, ...), condition=%wide.region_6.8_spmd, body=%wide.region_4.7_spmd.sunk | while | flops 524295 | bytes 5243093 | solution.py:25
  209.2 41.0 %all-gather.15.cloned.1.call-done = bf16[2048,256]{1,0:T(8,128)(2,1)} async-done(((bf16[256,256]{1,0:T(8,128)(2,1)}), bf16[2048,256]{1,0:T(8,128)(2,1)}) %all-gather.15.cloned.1.call-update) | async-done | bytes 1048592 | tf_op jit(solution)/shard_map/while/body/eval_jaxpr/all_gather | solution.py:9
  250.3 1.4 reduce_sum.40
  253.7 40.2 %all-gather.15.cloned.1.call-done = bf16[2048,256]{1,0:T(8,128)(2,1)} async-done(((bf16[256,256]{1,0:T(8,128)(2,1)}), bf16[2048,256]{1,0:T(8,128)(2,1)}) %all-gather.15.cloned.1.call-update) | async-done | bytes 1048592 | tf_op jit(solution)/shard_map/while/body/eval_jaxpr/all_gather | solution.py:9
  293.9 1.4 reduce_sum.40
  296.9 13.5 %all-reduce.10 = bf16[256,256]{1,0:T(8,128)(2,1)S(1)} all-reduce(f32[256,256]{1,0:T(8,128)S(1)} %bitcast.76), channel_id=1, replica_groups=mesh['row'=8,'rep'=4] {'rep'}, use_global_device_ids=true, to_apply=%region_7.9 | all-reduce | flops 65536 | bytes 393216 | tf_op jit(solution)/shard_map/psum | solution.py:40
  310.5 1.7 fusion.16
  312.2 17.7 %all-reduce.6.cloned.1.call-done = f32[256,256]{1,0:T(8,128)} async-done(((f32[256,256]{1,0:T(8,128)}), f32[256,256]{1,0:T(8,128)}) %all-reduce.6.cloned.1.call-update) | async-done | bytes 262160 | tf_op jit(solution)/shard_map/psum | solution.py:40
  329.9 1.8 fusion.15
  333.3 131.2 %all-reduce.8.cloned.1.call-done = (f32[256,256]{1,0:T(8,128)}, f32[256,256]{1,0:T(8,128)}) async-done(((f32[256,256]{1,0:T(8,128)}, f32[256,256]{1,0:T(8,128)}), (f32[256,256]{1,0:T(8,128)}, f32[256,256]{1,0:T(8,128)})) %all-reduce.8.cloned.1.call-update) | async-done | bytes 524304 | tf_op jit(solution)/shard_map/psum | solution.py:81
  464.5 1.7 copy.44
  (70 shorter events, 16.3 us)
Async XLA Ops:
  8.0 184.6 %copy-start = (bf16[1,1,2,4,128,128]{5,4,3,2,1,0:T(8,128)(2,1)S(1)}, bf16[1,1,2,4,128,128]{5,4,3,2,1,0:T(8,128)(2,1)}, u32[]{:S(2)}) copy-start(bf16[1,1,2,4,128,128]{5,4,3,2,1,0:T(8,128)(2,1)} %param.21) | copy-start | bytes 786436
  8.0 0.7 copy-start.4
  10.1 46.6 %all-gather.17.cloned.1.call-start = ((), (), s32[]{:S(2)}) async-start(), calls=%async_computation.4 | async-start | bytes 1179648 | tf_op jit(solution)/shard_map/while/body/eval_jaxpr/all_gather | solution.py:9
  58.1 42.5 %all-gather.17.cloned.1.call-start = ((), (), s32[]{:S(2)}) async-start(), calls=%async_computation.4 | async-start | bytes 1179648 | tf_op jit(solution)/shard_map/while/body/eval_jaxpr/all_gather | solution.py:9
  102.6 0.9 copy-start.1
  103.5 42.5 %all-gather.13.cloned.1.call-start = ((), (), s32[]{:S(2)}) async-start(), calls=%async_computation.2 | async-start | bytes 1179648 | tf_op jit(solution)/shard_map/while/body/eval_jaxpr/all_gather | solution.py:9
  147.4 42.2 %all-gather.13.cloned.1.call-start = ((), (), s32[]{:S(2)}) async-start(), calls=%async_computation.2 | async-start | bytes 1179648 | tf_op jit(solution)/shard_map/while/body/eval_jaxpr/all_gather | solution.py:9
  191.7 0.7 copy-start.6
  205.9 1.0 copy-start.5
  207.2 43.0 %all-gather.15.cloned.1.call-start = ((), (), s32[]{:S(2)}) async-start(), calls=%async_computation.3 | async-start | bytes 1179648 | tf_op jit(solution)/shard_map/while/body/eval_jaxpr/all_gather | solution.py:9
  251.7 42.2 %all-gather.15.cloned.1.call-start = ((), (), s32[]{:S(2)}) async-start(), calls=%async_computation.3 | async-start | bytes 1179648 | tf_op jit(solution)/shard_map/while/body/eval_jaxpr/all_gather | solution.py:9
  295.3 34.6 %all-reduce.6.cloned.1.call-start = ((), (), s32[]{:S(2)}) async-start(), calls=%async_computation | async-start | bytes 524288 | tf_op jit(solution)/shard_map/psum | solution.py:40
  295.9 168.6 %all-reduce.8.cloned.1.call-start = ((), (), s32[]{:S(2)}) async-start(), calls=%async_computation.1 | async-start | bytes 1048576 | tf_op jit(solution)/shard_map/psum | solution.py:81
  331.6 0.9 copy-start.2
  464.5 1.7 copy-start.3
Sparse Core Ops, SparseCore 0:
  13.6 42.9 all-gather.16
  61.6 38.9 all-gather.16
  107.0 38.9 all-gather.12
  150.6 38.9 all-gather.12
  210.5 39.7 all-gather.14
  254.9 38.9 all-gather.14
Sparse Core Ops, SparseCore 1:
  298.7 31.1 all-reduce.5
  335.8 128.7 all-reduce.7
